TPU v7x, 256 devices: a whole 4x4x8 slice. The times are simulated.
256 devices in a mesh: joint: 8 (over z), frame: 32 (over y, x, core).
Axes of the slice: x: 4, y: 4, z: 8, core: 2. Of those that a mesh axis runs over, the one named last changes fastest.
Arguments:
- tokens: bfloat16 [64, 768, 1536], P('joint', 'frame'), may hold values from -500 to 500
- norm_gain: float32 [1536], replicated, may hold values from 0.1 to 1.9
- qkv_weight: bfloat16 [1536, 3072], P('frame'), may hold values from -3 to 3
- out_grad: bfloat16 [64, 768, 1024], P('joint', 'frame'), may hold values from -6 to 6
Outputs:
- attended: bfloat16 [64, 768, 1024], P('joint', 'frame')
- token_grad: bfloat16 [64, 768, 1536], P('joint', 'frame')
- weight_grad: float32 [1536, 3072], P('frame')
- gain_grad: float32 [1536], replicated
All inputs are finite; a program needn't handle non-finite values.
Results may differ from a plain program's by a relative error of at most 0.029.
The roundings to bfloat16 on the way count: a program that leaves them out, or rounds other values in their place, can miss the bound.
Values may be sent and summed in bfloat16 or wider, within the bound.
No kernel may reach another device: no remote copies, remote signals or barrier semaphores. Data moves between devices by JAX's collectives and lax.ppermute only.
A program may use at most 128 MiB of HBM per device.

v0:
```python
import math
import jax
import jax.numpy as jnp
from jax import lax
from jax.sharding import PartitionSpec as P

HEADS = 8
HDIM = 128
EPSILON = 1e-05


def attention_local(queries, keys_all, values_all, upstream, inv_root, groups):
    scores = (
        jnp.einsum("fihd,fjhd->fhij", queries, keys_all, preferred_element_type=jnp.float32)
        * inv_root
    )
    probs = jax.nn.softmax(scores, axis=-1)
    probs_low = probs.astype(jnp.bfloat16)
    attended = jnp.einsum(
        "fhij,fjhd->fihd", probs_low, values_all, preferred_element_type=jnp.float32
    ).astype(jnp.bfloat16)
    prob_grad = jnp.einsum(
        "fihd,fjhd->fhij", upstream, values_all, preferred_element_type=jnp.float32
    )
    carried = jnp.sum(probs * prob_grad, axis=-1, keepdims=True)
    score_grad = (probs * (prob_grad - carried) * inv_root).astype(jnp.bfloat16)
    query_grad = jnp.einsum(
        "fhij,fjhd->fihd", score_grad, keys_all, preferred_element_type=jnp.float32
    ).astype(jnp.bfloat16)
    frames, joints = (queries.shape[0], queries.shape[1])
    size = joints // groups
    sg = score_grad.reshape(frames, HEADS, groups, size, joints)
    pl_ = probs_low.reshape(frames, HEADS, groups, size, joints)
    qg = queries.reshape(frames, groups, size, HEADS, HDIM)
    ug = upstream.reshape(frames, groups, size, HEADS, HDIM)
    key_part = jnp.einsum("fhgij,fgihd->fgjhd", sg, qg, preferred_element_type=jnp.float32)
    value_part = jnp.einsum("fhgij,fgihd->fgjhd", pl_, ug, preferred_element_type=jnp.float32)
    key_grad = jnp.sum(key_part.astype(jnp.bfloat16).astype(jnp.float32), axis=1).astype(
        jnp.bfloat16
    )
    value_grad = jnp.sum(value_part.astype(jnp.bfloat16).astype(jnp.float32), axis=1).astype(
        jnp.bfloat16
    )
    return (attended, query_grad, key_grad, value_grad)


def per_device(tokens, norm_gain, qkv_weight, out_grad):
    joint_rows, frame_rows, width = tokens.shape
    inner = out_grad.shape[2]
    joint_count = lax.axis_size("joint")
    total_tokens = joint_rows * frame_rows * joint_count * lax.axis_size("frame")
    grad_scale = 1.0 / math.sqrt(total_tokens)
    inv_root = 1.0 / math.sqrt(HDIM)
    joints = joint_rows * joint_count
    local_frames = frame_rows // joint_count
    count = joints * local_frames
    whole = lax.all_gather(qkv_weight, "frame", axis=0, tiled=True)
    packed = jnp.concatenate([tokens, out_grad], axis=2)
    packed = lax.all_to_all(packed, "joint", 1, 0, tiled=True)
    packed = packed.transpose(1, 0, 2)
    flat = packed[:, :, :width].reshape(count, width).astype(jnp.float32)
    upstream = packed[:, :, width:].reshape(local_frames, joints, HEADS, HDIM)
    rinv = lax.rsqrt(jnp.mean(flat * flat, axis=1, keepdims=True) + EPSILON)
    normed = flat * rinv
    scaled = (normed * norm_gain).astype(jnp.bfloat16)
    projected = jnp.dot(scaled, whole, preferred_element_type=jnp.float32).astype(jnp.bfloat16)
    projected = projected.reshape(local_frames, joints, 3, HEADS, HDIM)
    queries = projected[:, :, 0]
    keys_all = projected[:, :, 1]
    values_all = projected[:, :, 2]
    attended, query_grad, key_grad, value_grad = attention_local(
        queries, keys_all, values_all, upstream, inv_root, joint_count
    )
    qkv_grad = jnp.concatenate(
        [
            query_grad.reshape(count, inner),
            key_grad.reshape(count, inner),
            value_grad.reshape(count, inner),
        ],
        axis=1,
    )
    product = lax.dot_general(
        scaled, qkv_grad, (((0,), (0,)), ((), ())), preferred_element_type=jnp.float32
    )
    frame_sum = lax.psum_scatter(
        (product * grad_scale).astype(jnp.bfloat16), "frame", scatter_dimension=0, tiled=True
    )
    joint_part = lax.psum_scatter(frame_sum, "joint", scatter_dimension=1, tiled=True)
    weight_grad = lax.all_gather(joint_part, "joint", axis=1, tiled=True).astype(jnp.float32)
    normed_grad = lax.dot_general(
        qkv_grad, whole, (((1,), (1,)), ((), ())), preferred_element_type=jnp.float32
    )
    gain_part = jnp.sum(normed_grad * normed, axis=0) * grad_scale
    gain_grad = lax.psum(gain_part, ("joint", "frame"))
    upper = normed_grad * norm_gain
    token_grad = rinv * (upper - normed * jnp.mean(upper * normed, axis=1, keepdims=True))
    token_grad = token_grad.astype(jnp.bfloat16).reshape(local_frames, joints, width)
    back = jnp.concatenate(
        [attended.reshape(local_frames, joints, inner), token_grad], axis=2
    ).transpose(1, 0, 2)
    back = lax.all_to_all(back, "joint", 0, 1, tiled=True)
    attended_out = back[:, :, :inner]
    token_out = back[:, :, inner:]
    return (attended_out, token_out, weight_grad, gain_grad)


def solution(mesh):
    placed = (P("joint", "frame", None), P(), P("frame", None), P("joint", "frame", None))
    return jax.shard_map(
        per_device,
        mesh=mesh,
        in_specs=placed,
        out_specs=(P("joint", "frame", None), P("joint", "frame", None), P("frame", None), P()),
        check_vma=False,
    )
```

profile of v0, /device:TPU:32, one launch (start us, length us, event | category | flops | bytes accessed | tf_op | source)
XLA Modules:
  0.0 318.2 jit_solution(16296569881700968422)
XLA Ops:
  7.2 0.0 copy-start.4
  7.2 0.0 all-gather.2.cloned.1.call-start
  7.2 0.7 all-gather.2.cloned.1.call-update
  7.9 0.0 reduce-scatter.5.cloned.1.call-start
  8.0 1.2 copy.77
  9.2 0.2 copy.76
  9.4 0.1 pad_maximum_fusion
  9.4 34.2 %all_to_all.36 = bf16[8,24,2560]{2,0,1:T(8,128)(2,1)S(1)} all-to-all(bf16[8,24,2560]{2,0,1:T(8,128)(2,1)S(1)} %pad_maximum_fusion), channel_id=1, replica_groups=mesh['joint'=8,'frame'=32] {'joint'}, dimensions={1} | all-to-all | bytes 1966080 | tf_op jit(solution)/shard_map/all_to_all | solution.py:59
  43.7 0.1 copy.151
  43.8 0.2 multiply_reduce_fusion.2
  44.0 0.1 rsqrt.12
  44.1 0.1 slice_convert_fusion
  44.2 0.0 copy-start.9
  44.2 0.1 bitcast_multiply_fusion
  44.4 28.9 %all-gather.2.cloned.1.call-done = bf16[1536,3072]{1,0:T(8,128)(2,1)} async-done(((bf16[48,3072]{1,0:T(8,128)(2,1)}), bf16[1536,3072]{1,0:T(8,128)(2,1)}) %all-gather.2.cloned.1.call-update) | async-done | bytes 9437200 | tf_op jit(solution)/shard_map/all_gather | solution.py:57
  73.3 0.0 copy-done.9
  73.3 5.7 %fusion.3 = bf16[24,8,24,128]{3,1,2,0:T(8,128)(2,1)S(1)} fusion(bf16[1536,3072]{1,0:T(8,128)(2,1)} %all-gather.2.cloned.1.call-done, f32[192,1536]{1,0:T(8,128)S(1)} %bitcast_multiply_fusion, f32[1536]{0:T(1024)S(1)} %copy-done.9), kind=kOutput, calls=%fused_computation.7 | convolution fusion | flops 1813118976 | bytes 11802624 | tf_op jit(solution)/shard_map/dot_general | solution.py:66
  79.0 0.0 copy-done
  79.0 0.2 copy.111
  79.2 1.1 fusion.27
  80.3 0.3 fusion.12
  80.7 2.4 fusion.28
  83.1 2.7 fusion.10
  85.8 2.4 fusion.8
  88.2 0.1 fusion.26
  88.3 0.9 copy.91
  89.2 2.1 convert_reduce_fusion
  91.3 0.0 copy-start.5
  91.4 0.3 copy.93
  91.6 0.0 copy-done.7
  91.6 0.9 copy.87
  92.6 2.1 convert_reduce_fusion.1
  94.7 0.3 copy.90
  95.0 0.3 copy.86
  95.2 0.1 bitcast_dynamic-update-slice_fusion.2
  95.3 0.1 bitcast_dynamic-update-slice_fusion.1
  95.3 0.1 bitcast_dynamic-update-slice_fusion
  95.4 0.0 copy-start.8
  95.4 1.0 copy-done.8
  96.5 0.4 copy-done.1
  96.9 5.1 %multiply_convert_fusion = bf16[1536,3072]{1,0:T(8,128)(2,1)} fusion(bf16[192,3072]{1,0:T(8,128)(2,1)S(1)} %bitcast_dynamic-update-slice_fusion, f32[192,1536]{1,0:T(8,128)S(1)} %copy-done.1, f32[1536]{0:T(1024)S(1)} %copy-done.9), kind=kOutput, calls=%fused_computation.2 | convolution fusion | flops 1821966336 | bytes 11802624 | tf_op jit(solution)/shard_map/dot_general | solution.py:82
  102.0 0.0 reduce-scatter.5.cloned.1.call-update
  102.0 0.3 fusion.9
  102.3 0.3 copy.102
  102.6 0.1 reshape.73
  102.7 0.9 copy-done.2
  103.6 7.4 %multiply_reduce_fusion = (f32[1536]{0:T(1024)S(1)}, f32[192]{0:T(256)S(1)}, f32[192,1536]{1,0:T(8,128)S(1)}) fusion(f32[192,1536]{1,0:T(8,128)S(1)} %copy-done.2, f32[1536]{0:T(1024)S(1)} %copy-done.9, bf16[192,3072]{1,0:T(8,128)(2,1)} %copy-done.8, bf16[1536,3072]{1,0:T(8,128)(2,1)} %all-gather.2.cloned.1.call-done), kind=kOutput, calls=%fused_computation.20 | convolution fusion | flops 1813412096 | bytes 12989184 | tf_op jit(solution)/shard_map/dot_general | solution.py:90
  111.0 0.3 multiply_convert_fusion.1
  111.3 0.5 copy.95
  111.8 1.7 maximum_bitcast_fusion
  113.5 7.5 %all-to-all-start.1 = ((bf16[64,3,2560]{2,1,0:T(4,128)(2,1)}), bf16[64,3,2560]{2,1,0:T(4,128)(2,1)S(1)}, u32[]{:S(2)}, u32[]{:S(2)}) async-start(bf16[64,3,2560]{2,1,0:T(4,128)(2,1)} %maximum_bitcast_fusion), calls=%async_computation.1 | async-start | bytes 2621440 | tf_op jit(solution)/shard_map/all_to_all | solution.py:101
  121.0 0.0 reduce-scatter.7.cloned.1.call-start
  121.0 84.0 %reduce-scatter.5.cloned.1.call-done = bf16[48,3072]{1,0:T(8,128)(2,1)} async-done(((bf16[1536,3072]{1,0:T(8,128)(2,1)}), bf16[48,3072]{1,0:T(8,128)(2,1)}) %reduce-scatter.5.cloned.1.call-update) | async-done | bytes 294928 | tf_op jit(solution)/shard_map/reduce_scatter | solution.py:85
  204.9 2.2 copy.103
  207.1 0.0 reduce-scatter.7.cloned.1.call-update
  207.1 75.9 %psum.7 = f32[1536]{0:T(1024)} all-reduce(f32[1536]{0:T(1024)S(1)} %broadcast_multiply_fusion), channel_id=1, replica_groups=mesh['joint'=8,'frame'=32] {'joint','frame'}, use_global_device_ids=true, to_apply=%region_10.0 | all-reduce | flops 1536 | bytes 12288 | tf_op jit(solution)/shard_map/psum | solution.py:94
  283.1 0.0 all-to-all-done.1
  283.1 0.2 copy.150
  283.3 0.1 copy.97
  283.5 1.0 copy.99
  284.5 1.0 copy.98
  285.4 1.0 copy.104
  286.4 24.4 %all_gather.7 = bf16[48,3072]{1,0:T(8,128)(2,1)S(1)} all-gather(bf16[48,384]{1,0:T(8,128)(2,1)S(1)} %copy.104), channel_id=1, replica_groups=mesh['joint'=8,'frame'=32] {'joint'}, dimensions={1}, use_global_device_ids=true | all-gather | bytes 331776 | tf_op jit(solution)/shard_map/all_gather | solution.py:89
  310.8 0.9 convert_element_type.69
  (16 shorter events, 0.1 us)
Async XLA Ops:
  7.2 2.0 copy-start.4
  7.2 66.1 %all-gather.2.cloned.1.call-start = ((), (), s32[]{:S(2)}) async-start(), calls=%async_computation.4 | async-start | bytes 9732096 | tf_op jit(solution)/shard_map/all_gather | solution.py:57
  7.9 197.0 %reduce-scatter.5.cloned.1.call-start = ((), (), s32[]{:S(2)}) async-start(), calls=%async_computation.5 | async-start | bytes 9732096 | tf_op jit(solution)/shard_map/reduce_scatter | solution.py:85
  44.2 29.1 %copy-start.9 = (f32[1536]{0:T(1024)S(1)}, f32[1536]{0:T(1024)}, u32[]{:S(2)}) copy-start(f32[1536]{0:T(1024)} %param.5) | copy-start | bytes 18436
  44.4 34.6 %copy-start = (f32[192,1536]{1,0:T(8,128)}, f32[192,1536]{1,0:T(8,128)S(1)}, u32[]{:S(2)}) copy-start(f32[192,1536]{1,0:T(8,128)S(1)} %bitcast_multiply_fusion) | copy-start | bytes 3538948
  85.8 2.4 copy-start.3
  89.2 2.4 copy-start.7
  91.3 1.2 copy-start.5
  92.6 2.4 copy-start.6
  95.2 1.7 copy-start.1
  95.4 1.0 copy-start.8
  102.3 1.3 copy-start.2
  113.5 169.6 %all-to-all-start.1 = ((bf16[64,3,2560]{2,1,0:T(4,128)(2,1)}), bf16[64,3,2560]{2,1,0:T(4,128)(2,1)S(1)}, u32[]{:S(2)}, u32[]{:S(2)}) async-start(bf16[64,3,2560]{2,1,0:T(4,128)(2,1)} %maximum_bitcast_fusion), calls=%async_computation.1 | async-start | bytes 2621440 | tf_op jit(solution)/shard_map/all_to_all | solution.py:101
  121.0 164.5 %reduce-scatter.7.cloned.1.call-start = ((), (), s32[]{:S(2)}) async-start(), calls=%async_computation.6 | async-start | bytes 884736
Sparse Core Ops, SparseCore 0:
  10.5 62.7 all-gather.1
  102.1 102.7 reduce-scatter.4
  207.5 36.8 reduce-scatter.6
where the time goes:
time: 319 us; the launch traced here: 318 us
  blocking collectives  135 us (42%)
  waiting for transfers between devices  114 us (36%)
  matrix products  28.2 us (9%)
  local copies, waits for them, and re-layouts  14.4 us (5%)
  between operations  14 us (4%)
  starting transfers between devices  7.55 us (2%)
  other arithmetic  5.87 us (2%)
    reduce_scatter x1, waiting for transfers between devices, per_device(): lax.psum_scatter((product * grad_scale).astype(jnp.bfloat16), 'frame', sc...  84 us
    psum x1, blocking collectives, per_device(): gain_grad = lax.psum(gain_part, ('joint', 'frame'))  75.9 us
    all_to_all x1, blocking collectives, per_device(): packed = lax.all_to_all(packed, 'joint', 1, 0, tiled=True)  34.2 us
    all_gather x1, waiting for transfers between devices, per_device(): whole = lax.all_gather(qkv_weight, 'frame', axis=0, tiled=True)  28.9 us
    all_gather x1, blocking collectives, per_device(): lax.all_gather(joint_part, 'joint', axis=1, tiled=True).astype(jnp.float32)  24.4 us
    unnamed x29, local copies, waits for them, and re-layouts  9.18 us
    all_to_all x1, starting transfers between devices, per_device(): back = lax.all_to_all(back, 'joint', 0, 1, tiled=True)  7.47 us
    dot_general x1, matrix products, per_device(): lax.dot_general(qkv_grad, whole, (((1,), (1,)), ((), ())), preferred_elem...  7.44 us
  transfers between devices with their start and end apart: 4, of which 2 were waited for; matrix products, arithmetic and copies ran while one was open for 5% of the time, Pallas kernels for 0%

commit v1 on v0

--- a/solution.py
+++ b/solution.py
@@ -91,7 +91,7 @@
         qkv_grad, whole, (((1,), (1,)), ((), ())), preferred_element_type=jnp.float32
     )
     gain_part = jnp.sum(normed_grad * normed, axis=0) * grad_scale
-    gain_grad = lax.psum(gain_part, ("joint", "frame"))
+    gain_grad = jnp.sum(lax.all_gather(gain_part, ("joint", "frame")), axis=0)
     upper = normed_grad * norm_gain
     token_grad = rinv * (upper - normed * jnp.mean(upper * normed, axis=1, keepdims=True))
     token_grad = token_grad.astype(jnp.bfloat16).reshape(local_frames, joints, width)

time: 319 us -> 383 us (1.20)
  waiting for transfers between devices: 114 us -> 250 us
  blocking collectives: 135 us -> 59.1 us
  other arithmetic: 5.87 us -> 10.3 us
    all_gather x0 -> x1, waiting for transfers between devices: none -> 102 us  [per_device(): gain_grad = jnp.sum(lax.all_gather(gain_part, ('joint', 'frame')), axis=0)]
    psum x1 -> x0, blocking collectives: 75.9 us -> none  [per_device(): gain_grad = lax.psum(gain_part, ('joint', 'frame'))]
    unnamed x4 -> x5, waiting for transfers between devices: 0.72 us -> 37 us
    unnamed x29 -> x28, local copies, waits for them, and re-layouts: 9.18 us -> 9.4 us
  transfers between devices with their start and end apart: 4 -> 5, of which waited for: 2 -> 4; matrix products, arithmetic and copies ran while one was open for 5% -> 6% of each run, Pallas kernels for 0% -> 0%
where the time goes in v1:
time: 383 us; the launch traced here: 382 us
  waiting for transfers between devices  250 us (65%)
  blocking collectives  59.1 us (15%)
  matrix products  27.4 us (7%)
  between operations  14.1 us (4%)
  local copies, waits for them, and re-layouts  13.3 us (3%)
  other arithmetic  10.3 us (3%)
  starting transfers between devices  7.78 us (2%)
    all_gather x1, waiting for transfers between devices, per_device(): gain_grad = jnp.sum(lax.all_gather(gain_part, ('joint', 'frame')), axis=0)  102 us
    reduce_scatter x1, waiting for transfers between devices, per_device(): lax.psum_scatter((product * grad_scale).astype(jnp.bfloat16), 'frame', sc...  82.5 us
    unnamed x5, waiting for transfers between devices  37 us
    all_to_all x1, blocking collectives, per_device(): packed = lax.all_to_all(packed, 'joint', 1, 0, tiled=True)  34.2 us
    all_gather x1, waiting for transfers between devices, per_device(): whole = lax.all_gather(qkv_weight, 'frame', axis=0, tiled=True)  28 us
    all_gather x1, blocking collectives, per_device(): lax.all_gather(joint_part, 'joint', axis=1, tiled=True).astype(jnp.float32)  24.8 us
    unnamed x28, local copies, waits for them, and re-layouts  9.4 us
    dot_general x1, matrix products, per_device(): lax.dot_general(qkv_grad, whole, (((1,), (1,)), ((), ())), preferred_elem...  8.38 us
  transfers between devices with their start and end apart: 5, of which 4 were waited for; matrix products, arithmetic and copies ran while one was open for 6% of the time, Pallas kernels for 0%

profile of v1, /device:TPU:32, one launch (start us, length us, event | category | flops | bytes accessed | tf_op | source)
XLA Modules:
  0.0 381.5 jit_solution(14124280932670015126)
XLA Ops:
  7.2 0.0 all-gather.5.cloned.1.call-start
  7.2 0.7 all-gather.5.cloned.1.call-update
  7.9 0.0 reduce-scatter.5.cloned.1.call-start
  8.0 1.2 copy.77
  9.2 0.2 copy.76
  9.4 0.1 pad_maximum_fusion
  9.4 34.2 %all_to_all.36 = bf16[8,24,2560]{2,0,1:T(8,128)(2,1)S(1)} all-to-all(bf16[8,24,2560]{2,0,1:T(8,128)(2,1)S(1)} %pad_maximum_fusion), channel_id=1, replica_groups=mesh['joint'=8,'frame'=32] {'joint'}, dimensions={1} | all-to-all | bytes 1966080 | tf_op jit(solution)/shard_map/all_to_all | solution.py:59
  43.7 0.1 copy.151
  43.8 0.2 multiply_reduce_fusion.2
  44.0 0.1 rsqrt.12
  44.0 0.1 slice_convert_fusion
  44.2 0.0 copy-start.8
  44.2 1.1 bitcast_multiply_fusion
  45.3 28.0 %all-gather.5.cloned.1.call-done = bf16[1536,3072]{1,0:T(8,128)(2,1)} async-done(((bf16[48,3072]{1,0:T(8,128)(2,1)}), bf16[1536,3072]{1,0:T(8,128)(2,1)}) %all-gather.5.cloned.1.call-update) | async-done | bytes 9437200 | tf_op jit(solution)/shard_map/all_gather | solution.py:57
  73.3 6.1 %fusion.3 = bf16[24,8,24,128]{3,1,2,0:T(8,128)(2,1)S(1)} fusion(bf16[1536,3072]{1,0:T(8,128)(2,1)} %all-gather.5.cloned.1.call-done, f32[192,1536]{1,0:T(8,128)} %bitcast_multiply_fusion, f32[1536]{0:T(1024)S(1)} %copy-done.8), kind=kOutput, calls=%fused_computation.7 | convolution fusion | flops 1813118976 | bytes 11802624 | tf_op jit(solution)/shard_map/dot_general | solution.py:66
  79.4 0.2 copy.111
  79.6 0.2 fusion.27
  79.8 0.0 copy-start.4
  79.8 1.2 fusion.12
  81.1 1.3 fusion.28
  82.3 3.0 fusion.10
  85.4 2.9 fusion.8
  88.3 0.1 fusion.26
  88.4 0.2 copy.91
  88.6 1.0 convert_reduce_fusion
  89.6 0.0 copy-start.5
  89.6 0.3 copy.93
  89.9 1.2 copy.87
  91.1 0.0 copy-start.6
  91.1 1.0 convert_reduce_fusion.1
  92.2 0.3 copy.90
  92.5 0.3 copy.86
  92.7 0.1 bitcast_dynamic-update-slice_fusion.2
  92.8 0.1 bitcast_dynamic-update-slice_fusion.1
  92.8 0.1 bitcast_dynamic-update-slice_fusion
  92.9 1.0 copy-done.7
  94.0 0.4 copy-done
  94.4 5.1 %multiply_convert_fusion = bf16[1536,3072]{1,0:T(8,128)(2,1)} fusion(bf16[192,3072]{1,0:T(8,128)(2,1)S(1)} %bitcast_dynamic-update-slice_fusion, f32[192,1536]{1,0:T(8,128)S(1)} %copy-done, f32[1536]{0:T(1024)S(1)} %copy-done.8), kind=kOutput, calls=%fused_computation.2 | convolution fusion | flops 1821966336 | bytes 11802624 | tf_op jit(solution)/shard_map/dot_general | solution.py:82
  99.5 0.0 reduce-scatter.5.cloned.1.call-update
  99.5 0.2 all-gather.7.cloned.1.call-start
  99.7 8.4 %multiply_reduce_fusion = (f32[1536]{0:T(1024)S(1)}, f32[192]{0:T(256)S(1)}, f32[192,1536]{1,0:T(8,128)}) fusion(f32[192,1536]{1,0:T(8,128)S(1)} %copy-done, f32[1536]{0:T(1024)S(1)} %copy-done.8, bf16[192,3072]{1,0:T(8,128)(2,1)} %copy-done.7, bf16[1536,3072]{1,0:T(8,128)(2,1)} %all-gather.5.cloned.1.call-done), kind=kOutput, calls=%fused_computation.20 | convolution fusion | flops 1813412096 | bytes 12989184 | tf_op jit(solution)/shard_map/dot_general | solution.py:90
  108.1 0.6 reshape.83
  108.7 0.0 all-gather.7.cloned.1.call-update
  108.7 0.3 fusion.9
  109.1 0.3 copy.102
  109.3 0.1 reshape.86
  109.4 0.6 copy-done.1
  110.0 0.3 multiply_convert_fusion.1
  110.3 0.5 copy.95
  110.8 1.7 maximum_bitcast_fusion
  112.5 7.5 %all-to-all-start.1 = ((bf16[64,3,2560]{2,1,0:T(4,128)(2,1)}), bf16[64,3,2560]{2,1,0:T(4,128)(2,1)S(1)}, u32[]{:S(2)}, u32[]{:S(2)}) async-start(bf16[64,3,2560]{2,1,0:T(4,128)(2,1)} %maximum_bitcast_fusion), calls=%async_computation.1 | async-start | bytes 2621440 | tf_op jit(solution)/shard_map/all_to_all | solution.py:101
  119.9 82.5 %reduce-scatter.5.cloned.1.call-done = bf16[48,3072]{1,0:T(8,128)(2,1)} async-done(((bf16[1536,3072]{1,0:T(8,128)(2,1)}), bf16[48,3072]{1,0:T(8,128)(2,1)}) %reduce-scatter.5.cloned.1.call-update) | async-done | bytes 294928 | tf_op jit(solution)/shard_map/reduce_scatter | solution.py:85
  202.4 2.1 copy.103
  204.5 0.0 reduce-scatter.7.cloned.1.call-update
  204.6 0.2 copy.150
  204.8 0.1 copy.97
  205.0 1.0 copy.99
  206.0 1.0 copy.98
  206.9 102.2 %all-gather.7.cloned.1.call-done = f32[256,1,1536]{2,1,0:T(1,128)} async-done(((f32[1,1,1536]{2,1,0:T(1,128)}), f32[256,1,1536]{2,1,0:T(1,128)}) %all-gather.7.cloned.1.call-update) | async-done | bytes 1572880 | tf_op jit(solution)/shard_map/all_gather | solution.py:94
  309.1 2.9 reduce_sum.91
  312.0 36.3 %reduce-scatter.7.cloned.1.call-done = bf16[384,48]{1,0:T(8,128)(2,1)} async-done(((bf16[3072,48]{1,0:T(8,128)(2,1)}), bf16[384,48]{1,0:T(8,128)(2,1)}) %reduce-scatter.7.cloned.1.call-update) | async-done | bytes 36880
  348.3 1.0 copy.104
  349.3 24.8 %all_gather.11 = bf16[48,3072]{1,0:T(8,128)(2,1)S(1)} all-gather(bf16[48,384]{1,0:T(8,128)(2,1)S(1)} %copy.104), channel_id=1, replica_groups=mesh['joint'=8,'frame'=32] {'joint'}, dimensions={1}, use_global_device_ids=true | all-gather | bytes 331776 | tf_op jit(solution)/shard_map/all_gather | solution.py:89
  374.1 0.9 convert_element_type.69
  (18 shorter events, 0.1 us)
Async XLA Ops:
  7.2 2.0 copy-start.3
  7.2 66.1 %all-gather.5.cloned.1.call-start = ((), (), s32[]{:S(2)}) async-start(), calls=%async_computation.4 | async-start | bytes 9732096 | tf_op jit(solution)/shard_map/all_gather | solution.py:57
  7.9 194.5 %reduce-scatter.5.cloned.1.call-start = ((), (), s32[]{:S(2)}) async-start(), calls=%async_computation.5 | async-start | bytes 9732096 | tf_op jit(solution)/shard_map/reduce_scatter | solution.py:85
  44.2 29.1 %copy-start.8 = (f32[1536]{0:T(1024)S(1)}, f32[1536]{0:T(1024)}, u32[]{:S(2)}) copy-start(f32[1536]{0:T(1024)} %param.5) | copy-start | bytes 18436
  79.8 2.5 copy-start.4
  85.4 2.9 copy-start.2
  89.6 1.5 copy-start.5
  91.1 1.3 copy-start.6
  92.7 1.7 copy-start
  92.9 1.0 copy-start.7
  99.5 209.6 %all-gather.7.cloned.1.call-start = ((), (), s32[]{:S(2)}) async-start(), calls=%async_computation.6 | async-start | bytes 1579008 | tf_op jit(solution)/shard_map/all_gather | solution.py:94
  108.7 1.3 copy-start.1
  112.5 92.1 %all-to-all-start.1 = ((bf16[64,3,2560]{2,1,0:T(4,128)(2,1)}), bf16[64,3,2560]{2,1,0:T(4,128)(2,1)S(1)}, u32[]{:S(2)}, u32[]{:S(2)}) async-start(bf16[64,3,2560]{2,1,0:T(4,128)(2,1)} %maximum_bitcast_fusion), calls=%async_computation.1 | async-start | bytes 2621440 | tf_op jit(solution)/shard_map/all_to_all | solution.py:101
  119.9 228.4 %reduce-scatter.7.cloned.1.call-start = ((), (), s32[]{:S(2)}) async-start(), calls=%async_computation.7 | async-start | bytes 884736
Sparse Core Ops, SparseCore 0:
  10.5 62.7 all-gather.4
  99.6 102.7 reduce-scatter.4
  206.7 102.3 all-gather.6
  311.5 36.7 reduce-scatter.6
